TPU v7x, 32 devices: a whole 2x2x4 slice. The times are simulated.
32 devices in a mesh: sector: 8 (over y, x, core), sub: 4 (over z).
Axes of the slice: x: 2, y: 2, z: 4, core: 2. Of those that a mesh axis runs over, the one named last changes fastest.
Arguments:
- dual_load: float32 [8, 4, 2, 512, 256], P('sector', 'sub'), may hold values from -50 to 50
- flexibility: bfloat16 [8, 4, 2048, 2048], P('sector', 'sub'), may hold values from -10 to 10, as said below
- face_order: int32 [8, 4, 2048], P('sector', 'sub'), may hold values from 0 to 2047, each once within a row
- corner_index: int32 [8, 4, 32], P('sector', 'sub'), may hold values from 0 to 2047, as said below
- coarse_inverse: float32 [256, 256], replicated, may hold values from -10 to 10, as said below
Outputs:
- multiplier: float32 [8, 4, 2, 512, 256], P('sector', 'sub')
- residual: float32 [8, 4, 2, 512, 256], P('sector', 'sub')
Inputs may be any that keep to these rules, and one draw needn't show every extreme that they name: `flexibility`: a block of sizes of order one with a dominant diagonal; each subdomain's matrix is symmetric positive definite. `corner_index`: entries within one subdomain are distinct. `face_order`: each subdomain's row names every face slot once. `coarse_inverse`: symmetric positive definite with a dominant diagonal.
All inputs are finite; a program needn't handle non-finite values.
Results may differ from a plain program's by a relative error of at most 0.0087.
The roundings to bfloat16 on the way count: a program that leaves them out, or rounds other values in their place, can miss the bound.
Values may be sent and summed in bfloat16 or wider, within the bound.
No kernel may reach another device: no remote copies, remote signals or barrier semaphores. Data moves between devices by JAX's collectives and lax.ppermute only.
A program may use at most 128 MiB of HBM per device.

v0:
```python
import jax
import jax.numpy as jnp
from jax import lax
from jax.sharding import PartitionSpec as P

ITERS = 2


def passed_along(x, axis, by):
    count = lax.axis_size(axis)
    pairs = [(i, i + by) for i in range(count) if 0 <= i + by < count]
    return lax.ppermute(x, axis, pairs)


def from_behind(value, axis, steps):
    count = lax.axis_size(axis)
    pairs = [(source, (source + steps) % count) for source in range(count)]
    return lax.ppermute(value, axis, pairs)


def squares(residual):
    return lax.psum(jnp.sum(residual * residual, axis=(0, 1, 2, 3)), ("sector", "sub"))


def inner_sum(left, right):
    return jnp.sum(left * right, axis=(0, 1, 2, 3))


def shards(dual_load, flexibility, face_order, corner_index, coarse_inverse):
    slot_order = face_order[0, 0]
    corners = corner_index[0, 0]
    corner_count = corners.shape[0]
    slot_count = slot_order.shape[0]
    own_place = (
        jnp.zeros((slot_count,), jnp.int32)
        .at[slot_order]
        .set(jnp.arange(slot_count, dtype=jnp.int32))
    )
    matrix = flexibility[0, 0]
    face_width = slot_order.shape[0] // 4
    cases = dual_load.shape[-1]
    sub_count = lax.axis_size("sub")
    multiplier = jnp.zeros_like(dual_load)
    residual = dual_load
    direction = dual_load
    norm_now = squares(residual)
    for iteration in range(ITERS):
        rounded = direction[0, 0].astype(jnp.bfloat16)
        lower_sub = passed_along(rounded[0], "sub", 1)
        previous = from_behind(rounded[1], "sector", 1)
        face_stack = jnp.concatenate([-lower_sub, rounded[0], -previous, rounded[1]], axis=0)
        partial_value = jnp.take(face_stack, corners, axis=0).astype(jnp.float32)
        sector_total = lax.psum(partial_value.astype(jnp.bfloat16), "sub").astype(jnp.float32)
        sector_id = lax.axis_index("sector")
        everything = lax.all_gather(sector_total, "sector", axis=0, tiled=True)
        inverse_rows = lax.dynamic_slice_in_dim(
            coarse_inverse, sector_id * corner_count, corner_count, 0
        )
        coarse = jnp.dot(
            inverse_rows,
            everything,
            precision=lax.Precision.HIGHEST,
            preferred_element_type=jnp.float32,
        )
        coarse = coarse / sub_count
        correction = jnp.zeros((4 * face_width, cases), jnp.float32).at[corners].add(coarse)
        own_faces = jnp.take(face_stack, own_place, axis=0)
        own_product = jnp.dot(matrix, own_faces, preferred_element_type=jnp.float32)
        product = jnp.take(own_product, slot_order, axis=0) + correction
        outgoing_sub = product[:face_width]
        outgoing_cycle = product[2 * face_width : 3 * face_width]
        upper_next = passed_along(outgoing_sub.astype(jnp.bfloat16), "sub", -1)
        cycle_next = from_behind(outgoing_cycle.astype(jnp.bfloat16), "sector", -1)
        own_sub = product[face_width : 2 * face_width]
        own_cycle = product[3 * face_width :]
        jump_pair = jnp.stack(
            [own_sub - upper_next.astype(jnp.float32), own_cycle - cycle_next.astype(jnp.float32)],
            axis=0,
        )
        image = jump_pair[None, None]
        curvature = lax.psum(inner_sum(direction, image), ("sector", "sub"))
        alpha = norm_now / curvature
        multiplier = multiplier + alpha * direction
        residual = residual - alpha * image
        if iteration + 1 < ITERS:
            norm_next = squares(residual)
            direction = residual + norm_next / norm_now * direction
            norm_now = norm_next
    return (multiplier, residual)


def solution(mesh):
    return jax.shard_map(
        shards,
        mesh=mesh,
        in_specs=(
            P("sector", "sub", None, None, None),
            P("sector", "sub", None, None),
            P("sector", "sub", None),
            P("sector", "sub", None),
            P(),
        ),
        out_specs=(P("sector", "sub", None, None, None), P("sector", "sub", None, None, None)),
        check_vma=False,
    )
```

profile of v0, /device:TPU:10, one launch (start us, length us, event | category | flops | bytes accessed | tf_op | source)
XLA Modules:
  0.0 280.6 jit_solution(3341148262424951663)
XLA Ops:
  2.0 3.5 %collective-permute-start = (bf16[512,256]{1,0:T(8,128)(2,1)S(1)}, bf16[512,256]{1,0:T(8,128)(2,1)S(1)}, u32[]{:S(2)}, u32[]{:S(2)}) collective-permute-start(bf16[512,256]{1,0:T(8,128)(2,1)S(1)} %get-tuple-element.29), channel_id=1, source_target_pairs={{0,1},{1,2},{2,3},{4,5},{5,6},{6,7},{8,9},{9,10},{10,11},{12,13},{... | collective-permute-start | bytes 786440 | tf_op jit(solution)/shard_map/ppermute | solution.py:12
  5.7 8.0 %scatter_custom_fusion = s32[2048]{0:T(1024)S(1)} fusion(s32[2048]{0:T(1024)S(1)} %bitcast.66, s32[2048]{0:T(1024)S(1)} %iota.3, s32[]{:T(128)} %constant.11.clone.1), kind=kCustom, calls=%fused_computation.70 | custom fusion | bytes 8196 | tf_op jit(solution)/shard_map/scatter | solution.py:37
  14.6 7.5 %gather_fusion = bf16[2048,256]{1,0:T(8,128)(2,1)S(1)} fusion(bf16[2048,256]{1,0:T(8,128)(2,1)S(1)} %pad_maximum_fusion, s32[2048]{0:T(1024)S(1)} %fusion.33), kind=kCustom, calls=%fused_computation.clone | custom fusion | bytes 2105344 | tf_op jit(solution)/shard_map/jit(_take)/gather | solution.py:67
  22.2 14.2 %psum.43 = bf16[32,256]{1,0:T(8,128)(2,1)S(1)} all-reduce(bf16[32,256]{1,0:T(8,128)(2,1)S(1)} %broadcast_select_fusion.3), channel_id=1, replica_groups=mesh['sector'=8,'sub'=4] {'sub'}, use_global_device_ids=true, to_apply=%region_3.7 | all-reduce | flops 8192 | bytes 32768 | tf_op jit(solution)/shard_map/psum | solution.py:53
  36.5 9.3 %all_gather.6 = f32[256,256]{1,0:T(8,128)S(1)} all-gather(f32[32,256]{1,0:T(8,128)S(1)} %convert_element_type.35), channel_id=1, replica_groups=mesh['sector'=8,'sub'=4] {'sector'}, dimensions={0}, use_global_device_ids=true | all-gather | bytes 294912 | tf_op jit(solution)/shard_map/all_gather | solution.py:55
  45.8 7.5 %fusion.4 = f32[2048,256]{0,1:T(8,128)} fusion(bf16[1,1,2048,2048]{3,2,1,0:T(8,128)(2,1)} %param.12, bf16[2048,256]{1,0:T(8,128)(2,1)S(1)} %gather_fusion, pred[2048]{0:T(1024)(128)(4,1)S(1)} %compare_and_fusion.1), kind=kOutput, calls=%fused_computation.13 | convolution fusion | flops 2148007936 | bytes 11536384 | tf_op jit(solution)/shard_map/dot_general | solution.py:68
  53.3 1.9 copy.9
  55.2 8.6 %gather_fusion.1 = f32[2048,256]{1,0:T(8,128)} fusion(f32[2048,256]{1,0:T(8,128)S(1)} %copy.9, s32[2048]{0:T(1024)S(1)} %fusion.34), kind=kCustom, calls=%fused_computation.1.clone | custom fusion | bytes 4202496 | tf_op jit(solution)/shard_map/jit(_take)/gather | solution.py:69
  63.8 1.9 broadcast_select_fusion.1
  67.7 5.4 %collective-permute-start.2 = (bf16[512,256]{1,0:T(8,128)(2,1)S(1)}, bf16[512,256]{1,0:T(8,128)(2,1)S(1)}, u32[]{:S(2)}, u32[]{:S(2)}) collective-permute-start(bf16[512,256]{1,0:T(8,128)(2,1)S(1)} %get-tuple-element.25), channel_id=1, source_target_pairs={{1,0},{2,1},{3,2},{5,4},{6,5},{7,6},{9,8},{10,9},{11,10},{13,12},{... | collective-permute-start | bytes 786440 | tf_op jit(solution)/shard_map/ppermute | solution.py:12
  73.3 5.8 %collective-permute-done.2 = bf16[512,256]{1,0:T(8,128)(2,1)S(1)} collective-permute-done((bf16[512,256]{1,0:T(8,128)(2,1)S(1)}, bf16[512,256]{1,0:T(8,128)(2,1)S(1)}, u32[]{:S(2)}, u32[]{:S(2)}) %collective-permute-start.2) | collective-permute-done | bytes 262176 | tf_op jit(solution)/shard_map/ppermute | solution.py:12
  80.6 40.9 %all-reduce = (f32[256]{0:T(256)S(1)}, f32[256]{0:T(256)S(1)}) all-reduce(f32[256]{0:T(256)S(1)} %get-tuple-element.6, f32[256]{0:T(256)S(1)} %get-tuple-element.4), channel_id=1, replica_groups=mesh['sector'=8,'sub'=4] {'sector','sub'}, use_global_device_ids=true, to_apply=%region_1.0 | all-reduce | flops 512 | bytes 4096 | tf_op jit(solution)/shard_map/psum | solution.py:22
  121.7 39.4 %psum.45 = f32[256]{0:T(256)S(1)} all-reduce(f32[256]{0:T(256)S(1)} %multiply_reduce_fusion), channel_id=1, replica_groups=mesh['sector'=8,'sub'=4] {'sector','sub'}, use_global_device_ids=true, to_apply=%region_8.12 | all-reduce | flops 256 | bytes 2048 | tf_op jit(solution)/shard_map/psum | solution.py:22
  161.3 2.6 collective-permute-start.4
  164.0 5.6 %collective-permute-done.4 = bf16[512,256]{1,0:T(8,128)(2,1)S(1)} collective-permute-done((bf16[512,256]{1,0:T(8,128)(2,1)S(1)}, bf16[512,256]{1,0:T(8,128)(2,1)S(1)}, u32[]{:S(2)}, u32[]{:S(2)}) %collective-permute-start.4) | collective-permute-done | bytes 262176 | tf_op jit(solution)/shard_map/ppermute | solution.py:12
  170.5 7.5 %gather_fusion.3 = bf16[2048,256]{1,0:T(8,128)(2,1)S(1)} fusion(bf16[2048,256]{1,0:T(8,128)(2,1)S(1)} %pad_maximum_fusion.1, s32[2048]{0:T(1024)S(1)} %fusion.33), kind=kCustom, calls=%fused_computation.3.clone | custom fusion | bytes 2105344 | tf_op jit(solution)/shard_map/jit(_take)/gather | solution.py:67
  178.1 14.9 %psum.46 = bf16[32,256]{1,0:T(8,128)(2,1)S(1)} all-reduce(bf16[32,256]{1,0:T(8,128)(2,1)S(1)} %broadcast_select_fusion.2), channel_id=1, replica_groups=mesh['sector'=8,'sub'=4] {'sub'}, use_global_device_ids=true, to_apply=%region_9.13 | all-reduce | flops 8192 | bytes 32768 | tf_op jit(solution)/shard_map/psum | solution.py:53
  193.0 9.3 %all_gather.7 = f32[256,256]{1,0:T(8,128)S(1)} all-gather(f32[32,256]{1,0:T(8,128)S(1)} %convert_element_type.39), channel_id=1, replica_groups=mesh['sector'=8,'sub'=4] {'sector'}, dimensions={0}, use_global_device_ids=true | all-gather | bytes 294912 | tf_op jit(solution)/shard_map/all_gather | solution.py:55
  202.6 7.5 %fusion.7 = f32[2048,256]{0,1:T(8,128)} fusion(bf16[1,1,2048,2048]{3,2,1,0:T(8,128)(2,1)} %param.12, bf16[2048,256]{1,0:T(8,128)(2,1)S(1)} %gather_fusion.3, pred[2048]{0:T(1024)(128)(4,1)S(1)} %compare_and_fusion.1), kind=kOutput, calls=%fused_computation.14 | convolution fusion | flops 2148007936 | bytes 11536384 | tf_op jit(solution)/shard_map/dot_general | solution.py:68
  212.0 8.6 %gather_fusion.4 = f32[2048,256]{1,0:T(8,128)} fusion(f32[2048,256]{1,0:T(8,128)S(1)} %copy.10, s32[2048]{0:T(1024)S(1)} %fusion.34), kind=kCustom, calls=%fused_computation.4.clone | custom fusion | bytes 4202496 | tf_op jit(solution)/shard_map/jit(_take)/gather | solution.py:69
  220.6 1.9 broadcast_select_fusion
  224.3 6.1 %collective-permute-start.6 = (bf16[512,256]{1,0:T(8,128)(2,1)S(1)}, bf16[512,256]{1,0:T(8,128)(2,1)S(1)}, u32[]{:S(2)}, u32[]{:S(2)}) collective-permute-start(bf16[512,256]{1,0:T(8,128)(2,1)S(1)} %get-tuple-element.23), channel_id=1, source_target_pairs={{1,0},{2,1},{3,2},{5,4},{6,5},{7,6},{9,8},{10,9},{11,10},{13,12},{... | collective-permute-start | bytes 786440 | tf_op jit(solution)/shard_map/ppermute | solution.py:12
  230.7 5.7 %collective-permute-done.6 = bf16[512,256]{1,0:T(8,128)(2,1)S(1)} collective-permute-done((bf16[512,256]{1,0:T(8,128)(2,1)S(1)}, bf16[512,256]{1,0:T(8,128)(2,1)S(1)}, u32[]{:S(2)}, u32[]{:S(2)}) %collective-permute-start.6) | collective-permute-done | bytes 262176 | tf_op jit(solution)/shard_map/ppermute | solution.py:12
  237.9 41.0 %psum.47 = f32[256]{0:T(256)S(1)} all-reduce(f32[256]{0:T(256)S(1)} %fusion.14), channel_id=1, replica_groups=mesh['sector'=8,'sub'=4] {'sector','sub'}, use_global_device_ids=true, to_apply=%region_12.16 | all-reduce | flops 256 | bytes 2048 | tf_op jit(solution)/shard_map/psum | solution.py:81
  (77 shorter events, 14.6 us)
Async XLA Ops:
  0.6 65.1 %copy-start = (f32[256,256]{1,0:T(8,128)S(1)}, f32[256,256]{1,0:T(8,128)}, u32[]{:S(2)}) copy-start(f32[256,256]{1,0:T(8,128)} %param.15) | copy-start | bytes 786436
  0.6 4.9 %copy-start.11 = (s32[1,1,32]{2,1,0:T(1,128)S(1)}, s32[1,1,32]{2,1,0:T(1,128)}, u32[]{:S(2)}) copy-start(s32[1,1,32]{2,1,0:T(1,128)} %param.14) | copy-start | bytes 388
  0.7 5.0 %copy-start.10 = (s32[1,1,2048]{2,1,0:T(1,128)S(1)}, s32[1,1,2048]{2,1,0:T(1,128)}, u32[]{:S(2)}) copy-start(s32[1,1,2048]{2,1,0:T(1,128)} %param.13) | copy-start | bytes 24580
  2.0 11.8 %collective-permute-start = (bf16[512,256]{1,0:T(8,128)(2,1)S(1)}, bf16[512,256]{1,0:T(8,128)(2,1)S(1)}, u32[]{:S(2)}, u32[]{:S(2)}) collective-permute-start(bf16[512,256]{1,0:T(8,128)(2,1)S(1)} %get-tuple-element.29), channel_id=1, source_target_pairs={{0,1},{1,2},{2,3},{4,5},{5,6},{6,7},{8,9},{9,10},{10,11},{12,13},{... | collective-permute-start | bytes 786440 | tf_op jit(solution)/shard_map/ppermute | solution.py:12
  5.5 8.4 %collective-permute-start.1 = (bf16[512,256]{1,0:T(8,128)(2,1)S(1)}, bf16[512,256]{1,0:T(8,128)(2,1)S(1)}, u32[]{:S(2)}, u32[]{:S(2)}) collective-permute-start(bf16[512,256]{1,0:T(8,128)(2,1)S(1)} %get-tuple-element.30), channel_id=1, source_target_pairs={{0,4},{4,8},{8,12},{12,16},{16,20},{20,24},{24,28},{28,0},{1,5},{5... | collective-permute-start | bytes 786440 | tf_op jit(solution)/shard_map/ppermute | solution.py:18
  67.7 12.6 %copy-start.1 = (f32[1,1,2,512,256]{4,3,2,1,0:T(8,128)S(1)}, f32[1,1,2,512,256]{4,3,2,1,0:T(8,128)}, u32[]{:S(2)}) copy-start(f32[1,1,2,512,256]{4,3,2,1,0:T(8,128)} %param.11) | copy-start | bytes 3145732
  67.7 11.5 %collective-permute-start.2 = (bf16[512,256]{1,0:T(8,128)(2,1)S(1)}, bf16[512,256]{1,0:T(8,128)(2,1)S(1)}, u32[]{:S(2)}, u32[]{:S(2)}) collective-permute-start(bf16[512,256]{1,0:T(8,128)(2,1)S(1)} %get-tuple-element.25), channel_id=1, source_target_pairs={{1,0},{2,1},{3,2},{5,4},{6,5},{7,6},{9,8},{10,9},{11,10},{13,12},{... | collective-permute-start | bytes 786440 | tf_op jit(solution)/shard_map/ppermute | solution.py:12
  73.1 6.1 %collective-permute-start.3 = (bf16[512,256]{1,0:T(8,128)(2,1)S(1)}, bf16[512,256]{1,0:T(8,128)(2,1)S(1)}, u32[]{:S(2)}, u32[]{:S(2)}) collective-permute-start(bf16[512,256]{1,0:T(8,128)(2,1)S(1)} %get-tuple-element.26), channel_id=1, source_target_pairs={{0,28},{4,0},{8,4},{12,8},{16,12},{20,16},{24,20},{28,24},{1,29},{... | collective-permute-start | bytes 786440 | tf_op jit(solution)/shard_map/ppermute | solution.py:18
  80.3 41.2 %copy-start.2 = (f32[1,1,1,512,256]{4,3,2,1,0:T(8,128)S(1)}, f32[1,1,1,512,256]{4,3,2,1,0:T(8,128)}, u32[]{:S(2)}) copy-start(f32[1,1,1,512,256]{4,3,2,1,0:T(8,128)} %get-tuple-element.14) | copy-start | bytes 1572868
  80.3 41.2 %copy-start.5 = (f32[1,1,1,512,256]{4,3,2,1,0:T(8,128)S(1)}, f32[1,1,1,512,256]{4,3,2,1,0:T(8,128)}, u32[]{:S(2)}) copy-start(f32[1,1,1,512,256]{4,3,2,1,0:T(8,128)} %get-tuple-element.21) | copy-start | bytes 1572868
  161.3 8.3 %collective-permute-start.4 = (bf16[512,256]{1,0:T(8,128)(2,1)S(1)}, bf16[512,256]{1,0:T(8,128)(2,1)S(1)}, u32[]{:S(2)}, u32[]{:S(2)}) collective-permute-start(bf16[512,256]{1,0:T(8,128)(2,1)S(1)} %get-tuple-element.27), channel_id=1, source_target_pairs={{0,1},{1,2},{2,3},{4,5},{5,6},{6,7},{8,9},{9,10},{10,11},{12,13},{... | collective-permute-start | bytes 786440 | tf_op jit(solution)/shard_map/ppermute | solution.py:12
  163.9 5.8 %collective-permute-start.5 = (bf16[512,256]{1,0:T(8,128)(2,1)S(1)}, bf16[512,256]{1,0:T(8,128)(2,1)S(1)}, u32[]{:S(2)}, u32[]{:S(2)}) collective-permute-start(bf16[512,256]{1,0:T(8,128)(2,1)S(1)} %get-tuple-element.28), channel_id=1, source_target_pairs={{0,4},{4,8},{8,12},{12,16},{16,20},{20,24},{24,28},{28,0},{1,5},{5... | collective-permute-start | bytes 786440 | tf_op jit(solution)/shard_map/ppermute | solution.py:18
  224.2 13.4 %copy-start.3 = (f32[1,1,1,512,256]{4,3,2,1,0:T(8,128)S(1)}, f32[1,1,1,512,256]{4,3,2,1,0:T(8,128)}, u32[]{:S(2)}) copy-start(f32[1,1,1,512,256]{4,3,2,1,0:T(8,128)} %get-tuple-element.14) | copy-start | bytes 1572868
  224.2 13.4 %copy-start.6 = (f32[1,1,1,512,256]{4,3,2,1,0:T(8,128)S(1)}, f32[1,1,1,512,256]{4,3,2,1,0:T(8,128)}, u32[]{:S(2)}) copy-start(f32[1,1,1,512,256]{4,3,2,1,0:T(8,128)} %get-tuple-element.21) | copy-start | bytes 1572868
  224.3 12.2 %collective-permute-start.6 = (bf16[512,256]{1,0:T(8,128)(2,1)S(1)}, bf16[512,256]{1,0:T(8,128)(2,1)S(1)}, u32[]{:S(2)}, u32[]{:S(2)}) collective-permute-start(bf16[512,256]{1,0:T(8,128)(2,1)S(1)} %get-tuple-element.23), channel_id=1, source_target_pairs={{1,0},{2,1},{3,2},{5,4},{6,5},{7,6},{9,8},{10,9},{11,10},{13,12},{... | collective-permute-start | bytes 786440 | tf_op jit(solution)/shard_map/ppermute | solution.py:12
  230.4 6.1 %collective-permute-start.7 = (bf16[512,256]{1,0:T(8,128)(2,1)S(1)}, bf16[512,256]{1,0:T(8,128)(2,1)S(1)}, u32[]{:S(2)}, u32[]{:S(2)}) collective-permute-start(bf16[512,256]{1,0:T(8,128)(2,1)S(1)} %get-tuple-element.24), channel_id=1, source_target_pairs={{0,28},{4,0},{8,4},{12,8},{16,12},{20,16},{24,20},{28,24},{1,29},{... | collective-permute-start | bytes 786440 | tf_op jit(solution)/shard_map/ppermute | solution.py:18
  237.6 41.3 %copy-start.4 = (f32[1,1,1,512,256]{4,3,2,1,0:T(8,128)S(1)}, f32[1,1,1,512,256]{4,3,2,1,0:T(8,128)}, u32[]{:S(2)}) copy-start(f32[1,1,1,512,256]{4,3,2,1,0:T(8,128)} %get-tuple-element.14) | copy-start | bytes 1572868
  237.6 41.3 %copy-start.7 = (f32[1,1,1,512,256]{4,3,2,1,0:T(8,128)S(1)}, f32[1,1,1,512,256]{4,3,2,1,0:T(8,128)}, u32[]{:S(2)}) copy-start(f32[1,1,1,512,256]{4,3,2,1,0:T(8,128)} %get-tuple-element.21) | copy-start | bytes 1572868
  237.6 41.3 %copy-start.8 = (f32[1,1,1,512,256]{4,3,2,1,0:T(8,128)S(1)}, f32[1,1,1,512,256]{4,3,2,1,0:T(8,128)}, u32[]{:S(2)}) copy-start(f32[1,1,1,512,256]{4,3,2,1,0:T(8,128)} %get-tuple-element.9) | copy-start | bytes 1572868
  237.6 41.3 %copy-start.9 = (f32[1,1,1,512,256]{4,3,2,1,0:T(8,128)S(1)}, f32[1,1,1,512,256]{4,3,2,1,0:T(8,128)}, u32[]{:S(2)}) copy-start(f32[1,1,1,512,256]{4,3,2,1,0:T(8,128)} %get-tuple-element.20) | copy-start | bytes 1572868
where the time goes:
time: 281 us
  blocking collectives  169 us (60%)
  local copies, waits for them, and re-layouts  45.5 us (16%)
  starting transfers between devices  18.3 us (7%)
  waiting for transfers between devices  17.3 us (6%)
  matrix products  15.5 us (6%)
  other arithmetic  13.8 us (5%)
    psum x2, blocking collectives, squares(): lax.psum(jnp.sum(residual * residual, axis=(0, 1, 2, 3)), ('sector', 'sub'))  80.3 us
    psum x1, blocking collectives, shards(): curvature = lax.psum(inner_sum(direction, image), ('sector', 'sub'))  41 us
    psum x2, blocking collectives, shards(): lax.psum(partial_value.astype(jnp.bfloat16), 'sub').astype(jnp.float32)  29.2 us
    all_gather x2, blocking collectives, shards(): everything = lax.all_gather(sector_total, 'sector', axis=0, tiled=True)  18.6 us
    ppermute x4, starting transfers between devices, passed_along(): return lax.ppermute(x, axis, pairs)  17.6 us
    ppermute x4, waiting for transfers between devices, passed_along(): return lax.ppermute(x, axis, pairs)  17.2 us
    gather x2, local copies, waits for them, and re-layouts, shards(): product = jnp.take(own_product, slot_order, axis=0) + correction  17.1 us
    dot_general x2, matrix products, shards(): own_product = jnp.dot(matrix, own_faces, preferred_element_type=jnp.float32)  15 us
  transfers between devices with their start and end apart: 8, of which 4 were waited for; matrix products, arithmetic and copies ran while one was open for 3% of the time, Pallas kernels for 0%

commit v1 on v0

--- a/solution.py
+++ b/solution.py
@@ -4,6 +4,18 @@
 from jax.sharding import PartitionSpec as P
 
 ITERS = 2
+
+
+def collect(value, axis, dim):
+    ways, here = (lax.axis_size(axis), lax.axis_index(axis))
+    grown, reach = (value, 1)
+    while reach < ways:
+        theirs = lax.ppermute(grown, axis, [(d, d ^ reach) for d in range(ways)])
+        mine_first = jnp.concatenate([grown, theirs], axis=dim)
+        theirs_first = jnp.concatenate([theirs, grown], axis=dim)
+        grown = jnp.where(here & reach == 0, mine_first, theirs_first)
+        reach = 2 * reach
+    return grown
 
 
 def passed_along(x, axis, by):
@@ -52,7 +64,7 @@
         partial_value = jnp.take(face_stack, corners, axis=0).astype(jnp.float32)
         sector_total = lax.psum(partial_value.astype(jnp.bfloat16), "sub").astype(jnp.float32)
         sector_id = lax.axis_index("sector")
-        everything = lax.all_gather(sector_total, "sector", axis=0, tiled=True)
+        everything = collect(sector_total, "sector", 0)
         inverse_rows = lax.dynamic_slice_in_dim(
             coarse_inverse, sector_id * corner_count, corner_count, 0
         )

time: 281 us -> 272 us (0.968)
  blocking collectives: 169 us -> 152 us
  starting transfers between devices: 18.3 us -> 22.8 us
    all_gather x2 -> x0, blocking collectives: 18.6 us -> none  [shards(): everything = lax.all_gather(sector_total, 'sector', axis=0, tiled=True)]
    ppermute x0 -> x6, starting transfers between devices: none -> 5.37 us  [collect(): theirs = lax.ppermute(grown, axis, [(d, d ^ reach) for d in range(ways)])]
    ppermute x0 -> x6, waiting for transfers between devices: none -> 4.07 us  [collect(): theirs = lax.ppermute(grown, axis, [(d, d ^ reach) for d in range(ways)])]
  transfers between devices with their start and end apart: 8 -> 14, of which waited for: 4 -> 6; matrix products, arithmetic and copies ran while one was open for 3% -> 23% of each run, Pallas kernels for 0% -> 0%
where the time goes in v1:
time: 272 us
  blocking collectives  152 us (56%)
  local copies, waits for them, and re-layouts  45.6 us (17%)
  starting transfers between devices  22.8 us (8%)
  waiting for transfers between devices  19.5 us (7%)
  matrix products  15.5 us (6%)
  other arithmetic  14.8 us (5%)
    psum x2, blocking collectives, squares(): lax.psum(jnp.sum(residual * residual, axis=(0, 1, 2, 3)), ('sector', 'sub'))  81.3 us
    psum x1, blocking collectives, shards(): curvature = lax.psum(inner_sum(direction, image), ('sector', 'sub'))  41.8 us
    psum x2, blocking collectives, shards(): lax.psum(partial_value.astype(jnp.bfloat16), 'sub').astype(jnp.float32)  29.2 us
    gather x2, local copies, waits for them, and re-layouts, shards(): product = jnp.take(own_product, slot_order, axis=0) + correction  17.2 us
    ppermute x4, starting transfers between devices, passed_along(): return lax.ppermute(x, axis, pairs)  17 us
    ppermute x4, waiting for transfers between devices, passed_along(): return lax.ppermute(x, axis, pairs)  15.4 us
    dot_general x2, matrix products, shards(): own_product = jnp.dot(matrix, own_faces, preferred_element_type=jnp.float32)  15 us
    gather x2, local copies, waits for them, and re-layouts, shards(): own_faces = jnp.take(face_stack, own_place, axis=0)  15 us
  transfers between devices with their start and end apart: 14, of which 6 were waited for; matrix products, arithmetic and copies ran while one was open for 23% of the time, Pallas kernels for 0%

profile of v1, /device:TPU:10, one launch (start us, length us, event | category | flops | bytes accessed | tf_op | source)
XLA Modules:
  0.0 271.7 jit_solution(6558979093125296109)
XLA Ops:
  2.0 3.5 %collective-permute-start = (bf16[512,256]{1,0:T(8,128)(2,1)S(1)}, bf16[512,256]{1,0:T(8,128)(2,1)S(1)}, u32[]{:S(2)}, u32[]{:S(2)}) collective-permute-start(bf16[512,256]{1,0:T(8,128)(2,1)S(1)} %get-tuple-element.29), channel_id=1, source_target_pairs={{0,1},{1,2},{2,3},{4,5},{5,6},{6,7},{8,9},{9,10},{10,11},{12,13},{... | collective-permute-start | bytes 786440 | tf_op jit(solution)/shard_map/ppermute | solution.py:24
  5.7 8.0 %scatter_custom_fusion = s32[2048]{0:T(1024)S(1)} fusion(s32[2048]{0:T(1024)S(1)} %bitcast.64, s32[2048]{0:T(1024)S(1)} %iota.3, s32[]{:T(128)} %constant.6.clone.1), kind=kCustom, calls=%fused_computation.88 | custom fusion | bytes 8196 | tf_op jit(solution)/shard_map/scatter | solution.py:49
  14.7 14.2 %psum.43 = bf16[32,256]{1,0:T(8,128)(2,1)S(1)} all-reduce(bf16[32,256]{1,0:T(8,128)(2,1)S(1)} %broadcast_select_fusion.3), channel_id=1, replica_groups=mesh['sector'=8,'sub'=4] {'sub'}, use_global_device_ids=true, to_apply=%region_3.7 | all-reduce | flops 8192 | bytes 32768 | tf_op jit(solution)/shard_map/psum | solution.py:65
  29.1 7.5 %gather_fusion = bf16[2048,256]{1,0:T(8,128)(2,1)S(1)} fusion(bf16[2048,256]{1,0:T(8,128)(2,1)S(1)} %pad_maximum_fusion, s32[2048]{0:T(1024)S(1)} %fusion.45), kind=kCustom, calls=%fused_computation.clone | custom fusion | bytes 2105344 | tf_op jit(solution)/shard_map/jit(_take)/gather | solution.py:79
  37.2 7.5 %fusion.4 = f32[2048,256]{0,1:T(8,128)} fusion(bf16[1,1,2048,2048]{3,2,1,0:T(8,128)(2,1)} %param.12, bf16[2048,256]{1,0:T(8,128)(2,1)S(1)} %gather_fusion, pred[2048]{0:T(1024)(128)(4,1)S(1)} %compare_and_fusion.1), kind=kOutput, calls=%fused_computation.13 | convolution fusion | flops 2148007936 | bytes 11536384 | tf_op jit(solution)/shard_map/dot_general | solution.py:80
  46.6 8.6 %gather_fusion.1 = f32[2048,256]{1,0:T(8,128)} fusion(f32[2048,256]{1,0:T(8,128)S(1)} %copy.9, s32[2048]{0:T(1024)S(1)} %fusion.46), kind=kCustom, calls=%fused_computation.1.clone | custom fusion | bytes 4202496 | tf_op jit(solution)/shard_map/jit(_take)/gather | solution.py:81
  56.8 1.9 broadcast_select_fusion.1
  58.8 2.1 collective-permute-done.4
  62.9 5.4 %collective-permute-start.5 = (bf16[512,256]{1,0:T(8,128)(2,1)S(1)}, bf16[512,256]{1,0:T(8,128)(2,1)S(1)}, u32[]{:S(2)}, u32[]{:S(2)}) collective-permute-start(bf16[512,256]{1,0:T(8,128)(2,1)S(1)} %get-tuple-element.25), channel_id=1, source_target_pairs={{1,0},{2,1},{3,2},{5,4},{6,5},{7,6},{9,8},{10,9},{11,10},{13,12},{... | collective-permute-start | bytes 786440 | tf_op jit(solution)/shard_map/ppermute | solution.py:24
  68.5 4.8 %collective-permute-done.5 = bf16[512,256]{1,0:T(8,128)(2,1)S(1)} collective-permute-done((bf16[512,256]{1,0:T(8,128)(2,1)S(1)}, bf16[512,256]{1,0:T(8,128)(2,1)S(1)}, u32[]{:S(2)}, u32[]{:S(2)}) %collective-permute-start.5) | collective-permute-done | bytes 262176 | tf_op jit(solution)/shard_map/ppermute | solution.py:24
  74.7 41.9 %all-reduce = (f32[256]{0:T(256)S(1)}, f32[256]{0:T(256)S(1)}) all-reduce(f32[256]{0:T(256)S(1)} %get-tuple-element.6, f32[256]{0:T(256)S(1)} %get-tuple-element.4), channel_id=1, replica_groups=mesh['sector'=8,'sub'=4] {'sector','sub'}, use_global_device_ids=true, to_apply=%region_1.0 | all-reduce | flops 512 | bytes 4096 | tf_op jit(solution)/shard_map/psum | solution.py:34
  116.8 39.4 %psum.45 = f32[256]{0:T(256)S(1)} all-reduce(f32[256]{0:T(256)S(1)} %multiply_reduce_fusion), channel_id=1, replica_groups=mesh['sector'=8,'sub'=4] {'sector','sub'}, use_global_device_ids=true, to_apply=%region_8.12 | all-reduce | flops 256 | bytes 2048 | tf_op jit(solution)/shard_map/psum | solution.py:34
  156.5 2.6 collective-permute-start.7
  159.1 5.6 %collective-permute-done.7 = bf16[512,256]{1,0:T(8,128)(2,1)S(1)} collective-permute-done((bf16[512,256]{1,0:T(8,128)(2,1)S(1)}, bf16[512,256]{1,0:T(8,128)(2,1)S(1)}, u32[]{:S(2)}, u32[]{:S(2)}) %collective-permute-start.7) | collective-permute-done | bytes 262176 | tf_op jit(solution)/shard_map/ppermute | solution.py:24
  165.7 15.0 %psum.46 = bf16[32,256]{1,0:T(8,128)(2,1)S(1)} all-reduce(bf16[32,256]{1,0:T(8,128)(2,1)S(1)} %broadcast_select_fusion.2), channel_id=1, replica_groups=mesh['sector'=8,'sub'=4] {'sub'}, use_global_device_ids=true, to_apply=%region_9.13 | all-reduce | flops 8192 | bytes 32768 | tf_op jit(solution)/shard_map/psum | solution.py:65
  180.8 7.5 %gather_fusion.3 = bf16[2048,256]{1,0:T(8,128)(2,1)S(1)} fusion(bf16[2048,256]{1,0:T(8,128)(2,1)S(1)} %pad_maximum_fusion.1, s32[2048]{0:T(1024)S(1)} %fusion.45), kind=kCustom, calls=%fused_computation.3.clone | custom fusion | bytes 2105344 | tf_op jit(solution)/shard_map/jit(_take)/gather | solution.py:79
  189.0 7.5 %fusion.7 = f32[2048,256]{0,1:T(8,128)} fusion(bf16[1,1,2048,2048]{3,2,1,0:T(8,128)(2,1)} %param.12, bf16[2048,256]{1,0:T(8,128)(2,1)S(1)} %gather_fusion.3, pred[2048]{0:T(1024)(128)(4,1)} %copy-done.17), kind=kOutput, calls=%fused_computation.14 | convolution fusion | flops 2148007936 | bytes 11536384 | tf_op jit(solution)/shard_map/dot_general | solution.py:80
  198.4 8.6 %gather_fusion.4 = f32[2048,256]{1,0:T(8,128)} fusion(f32[2048,256]{1,0:T(8,128)S(1)} %copy.10, s32[2048]{0:T(1024)S(1)} %fusion.46), kind=kCustom, calls=%fused_computation.4.clone | custom fusion | bytes 4202496 | tf_op jit(solution)/shard_map/jit(_take)/gather | solution.py:81
  208.0 2.3 collective-permute-start.11
  210.3 1.9 broadcast_select_fusion
  212.2 1.9 collective-permute-done.11
  216.2 5.5 %collective-permute-start.12 = (bf16[512,256]{1,0:T(8,128)(2,1)S(1)}, bf16[512,256]{1,0:T(8,128)(2,1)S(1)}, u32[]{:S(2)}, u32[]{:S(2)}) collective-permute-start(bf16[512,256]{1,0:T(8,128)(2,1)S(1)} %get-tuple-element.23), channel_id=1, source_target_pairs={{1,0},{2,1},{3,2},{5,4},{6,5},{7,6},{9,8},{10,9},{11,10},{13,12},{... | collective-permute-start | bytes 786440 | tf_op jit(solution)/shard_map/ppermute | solution.py:24
  221.8 4.9 %collective-permute-done.12 = bf16[512,256]{1,0:T(8,128)(2,1)S(1)} collective-permute-done((bf16[512,256]{1,0:T(8,128)(2,1)S(1)}, bf16[512,256]{1,0:T(8,128)(2,1)S(1)}, u32[]{:S(2)}, u32[]{:S(2)}) %collective-permute-start.12) | collective-permute-done | bytes 262176 | tf_op jit(solution)/shard_map/ppermute | solution.py:24
  228.2 41.8 %psum.47 = f32[256]{0:T(256)S(1)} all-reduce(f32[256]{0:T(256)S(1)} %fusion.14), channel_id=1, replica_groups=mesh['sector'=8,'sub'=4] {'sector','sub'}, use_global_device_ids=true, to_apply=%region_12.16 | all-reduce | flops 256 | bytes 2048 | tf_op jit(solution)/shard_map/psum | solution.py:93
  (105 shorter events, 20.3 us)
Async XLA Ops:
  0.6 60.3 %copy-start = (f32[256,256]{1,0:T(8,128)S(1)}, f32[256,256]{1,0:T(8,128)}, u32[]{:S(2)}) copy-start(f32[256,256]{1,0:T(8,128)} %param.15) | copy-start | bytes 786436
  2.0 11.8 %collective-permute-start = (bf16[512,256]{1,0:T(8,128)(2,1)S(1)}, bf16[512,256]{1,0:T(8,128)(2,1)S(1)}, u32[]{:S(2)}, u32[]{:S(2)}) collective-permute-start(bf16[512,256]{1,0:T(8,128)(2,1)S(1)} %get-tuple-element.29), channel_id=1, source_target_pairs={{0,1},{1,2},{2,3},{4,5},{5,6},{6,7},{8,9},{9,10},{10,11},{12,13},{... | collective-permute-start | bytes 786440 | tf_op jit(solution)/shard_map/ppermute | solution.py:24
  5.5 8.3 %collective-permute-start.1 = (bf16[512,256]{1,0:T(8,128)(2,1)S(1)}, bf16[512,256]{1,0:T(8,128)(2,1)S(1)}, u32[]{:S(2)}, u32[]{:S(2)}) collective-permute-start(bf16[512,256]{1,0:T(8,128)(2,1)S(1)} %get-tuple-element.30), channel_id=1, source_target_pairs={{0,4},{4,8},{8,12},{12,16},{16,20},{20,24},{24,28},{28,0},{1,5},{5... | collective-permute-start | bytes 786440 | tf_op jit(solution)/shard_map/ppermute | solution.py:30
  13.8 23.4 %copy-start.17 = (pred[2048]{0:T(1024)(128)(4,1)}, pred[2048]{0:T(1024)(128)(4,1)S(1)}, u32[]{:S(2)}) copy-start(pred[2048]{0:T(1024)(128)(4,1)S(1)} %compare_and_fusion.1) | copy-start | bytes 6148
  28.9 7.6 %collective-permute-start.2 = (f32[32,256]{1,0:T(8,128)S(1)}, f32[32,256]{1,0:T(8,128)S(1)}, u32[]{:S(2)}, u32[]{:S(2)}) collective-permute-start(f32[32,256]{1,0:T(8,128)S(1)} %convert_element_type.35), channel_id=1, source_target_pairs={{0,4},{4,0},{8,12},{12,8},{16,20},{20,16},{24,28},{28,24},{1,5},{5... | collective-permute-start | bytes 98312 | tf_op jit(solution)/shard_map/ppermute | solution.py:13
  29.0 32.1 %copy-start.15 = (s32[32]{0:T(128)}, s32[32]{0:T(128)S(1)}, u32[]{:S(2)}) copy-start(s32[32]{0:T(128)S(1)} %fusion.49) | copy-start | bytes 388
  36.6 18.6 %collective-permute-start.3 = (f32[64,256]{1,0:T(8,128)S(1)}, f32[64,256]{1,0:T(8,128)S(1)}, u32[]{:S(2)}, u32[]{:S(2)}) collective-permute-start(f32[64,256]{1,0:T(8,128)S(1)} %maximum_select_fusion.6), channel_id=1, source_target_pairs={{0,8},{4,12},{8,0},{12,4},{16,24},{20,28},{24,16},{28,20},{1,9},{5... | collective-permute-start | bytes 196616 | tf_op jit(solution)/shard_map/ppermute | solution.py:13
  55.2 5.6 %collective-permute-start.4 = (f32[128,256]{1,0:T(8,128)S(1)}, f32[128,256]{1,0:T(8,128)S(1)}, u32[]{:S(2)}, u32[]{:S(2)}) collective-permute-start(f32[128,256]{1,0:T(8,128)S(1)} %maximum_select_fusion.4), channel_id=1, source_target_pairs={{0,16},{4,20},{8,24},{12,28},{16,0},{20,4},{24,8},{28,12},{1,17},{... | collective-permute-start | bytes 393224 | tf_op jit(solution)/shard_map/ppermute | solution.py:13
  62.9 10.4 %collective-permute-start.5 = (bf16[512,256]{1,0:T(8,128)(2,1)S(1)}, bf16[512,256]{1,0:T(8,128)(2,1)S(1)}, u32[]{:S(2)}, u32[]{:S(2)}) collective-permute-start(bf16[512,256]{1,0:T(8,128)(2,1)S(1)} %get-tuple-element.25), channel_id=1, source_target_pairs={{1,0},{2,1},{3,2},{5,4},{6,5},{7,6},{9,8},{10,9},{11,10},{13,12},{... | collective-permute-start | bytes 786440 | tf_op jit(solution)/shard_map/ppermute | solution.py:24
  68.3 5.0 %collective-permute-start.6 = (bf16[512,256]{1,0:T(8,128)(2,1)S(1)}, bf16[512,256]{1,0:T(8,128)(2,1)S(1)}, u32[]{:S(2)}, u32[]{:S(2)}) collective-permute-start(bf16[512,256]{1,0:T(8,128)(2,1)S(1)} %get-tuple-element.26), channel_id=1, source_target_pairs={{0,28},{4,0},{8,4},{12,8},{16,12},{20,16},{24,20},{28,24},{1,29},{... | collective-permute-start | bytes 786440 | tf_op jit(solution)/shard_map/ppermute | solution.py:30
  74.4 42.2 %copy-start.2 = (f32[1,1,1,512,256]{4,3,2,1,0:T(8,128)S(1)}, f32[1,1,1,512,256]{4,3,2,1,0:T(8,128)}, u32[]{:S(2)}) copy-start(f32[1,1,1,512,256]{4,3,2,1,0:T(8,128)} %get-tuple-element.14) | copy-start | bytes 1572868
  74.4 42.2 %copy-start.5 = (f32[1,1,1,512,256]{4,3,2,1,0:T(8,128)S(1)}, f32[1,1,1,512,256]{4,3,2,1,0:T(8,128)}, u32[]{:S(2)}) copy-start(f32[1,1,1,512,256]{4,3,2,1,0:T(8,128)} %get-tuple-element.21) | copy-start | bytes 1572868
  156.5 8.3 %collective-permute-start.7 = (bf16[512,256]{1,0:T(8,128)(2,1)S(1)}, bf16[512,256]{1,0:T(8,128)(2,1)S(1)}, u32[]{:S(2)}, u32[]{:S(2)}) collective-permute-start(bf16[512,256]{1,0:T(8,128)(2,1)S(1)} %get-tuple-element.27), channel_id=1, source_target_pairs={{0,1},{1,2},{2,3},{4,5},{5,6},{6,7},{8,9},{9,10},{10,11},{12,13},{... | collective-permute-start | bytes 786440 | tf_op jit(solution)/shard_map/ppermute | solution.py:24
  159.0 5.8 %collective-permute-start.8 = (bf16[512,256]{1,0:T(8,128)(2,1)S(1)}, bf16[512,256]{1,0:T(8,128)(2,1)S(1)}, u32[]{:S(2)}, u32[]{:S(2)}) collective-permute-start(bf16[512,256]{1,0:T(8,128)(2,1)S(1)} %get-tuple-element.28), channel_id=1, source_target_pairs={{0,4},{4,8},{8,12},{12,16},{16,20},{20,24},{24,28},{28,0},{1,5},{5... | collective-permute-start | bytes 786440 | tf_op jit(solution)/shard_map/ppermute | solution.py:30
  180.7 7.6 %collective-permute-start.9 = (f32[32,256]{1,0:T(8,128)S(1)}, f32[32,256]{1,0:T(8,128)S(1)}, u32[]{:S(2)}, u32[]{:S(2)}) collective-permute-start(f32[32,256]{1,0:T(8,128)S(1)} %convert_element_type.39), channel_id=1, source_target_pairs={{0,4},{4,0},{8,12},{12,8},{16,20},{20,16},{24,28},{28,24},{1,5},{5... | collective-permute-start | bytes 98312 | tf_op jit(solution)/shard_map/ppermute | solution.py:13
  188.3 18.7 %collective-permute-start.10 = (f32[64,256]{1,0:T(8,128)S(1)}, f32[64,256]{1,0:T(8,128)}, u32[]{:S(2)}, u32[]{:S(2)}) collective-permute-start(f32[64,256]{1,0:T(8,128)S(1)} %maximum_select_fusion.7), channel_id=1, source_target_pairs={{0,8},{4,12},{8,0},{12,4},{16,24},{20,28},{24,16},{28,20},{1,9},{5... | collective-permute-start | bytes 196616 | tf_op jit(solution)/shard_map/ppermute | solution.py:13
  208.0 6.2 %collective-permute-start.11 = (f32[128,256]{1,0:T(8,128)S(1)}, f32[128,256]{1,0:T(8,128)S(1)}, u32[]{:S(2)}, u32[]{:S(2)}) collective-permute-start(f32[128,256]{1,0:T(8,128)S(1)} %maximum_select_fusion.5), channel_id=1, source_target_pairs={{0,16},{4,20},{8,24},{12,28},{16,0},{20,4},{24,8},{28,12},{1,17},{... | collective-permute-start | bytes 393224 | tf_op jit(solution)/shard_map/ppermute | solution.py:13
  216.2 10.6 %collective-permute-start.12 = (bf16[512,256]{1,0:T(8,128)(2,1)S(1)}, bf16[512,256]{1,0:T(8,128)(2,1)S(1)}, u32[]{:S(2)}, u32[]{:S(2)}) collective-permute-start(bf16[512,256]{1,0:T(8,128)(2,1)S(1)} %get-tuple-element.23), channel_id=1, source_target_pairs={{1,0},{2,1},{3,2},{5,4},{6,5},{7,6},{9,8},{10,9},{11,10},{13,12},{... | collective-permute-start | bytes 786440 | tf_op jit(solution)/shard_map/ppermute | solution.py:24
  221.7 5.1 %collective-permute-start.13 = (bf16[512,256]{1,0:T(8,128)(2,1)S(1)}, bf16[512,256]{1,0:T(8,128)(2,1)S(1)}, u32[]{:S(2)}, u32[]{:S(2)}) collective-permute-start(bf16[512,256]{1,0:T(8,128)(2,1)S(1)} %get-tuple-element.24), channel_id=1, source_target_pairs={{0,28},{4,0},{8,4},{12,8},{16,12},{20,16},{24,20},{28,24},{1,29},{... | collective-permute-start | bytes 786440 | tf_op jit(solution)/shard_map/ppermute | solution.py:30
  227.9 42.1 %copy-start.14 = (f32[256]{0:T(256)S(1)}, f32[256]{0:T(256)}, u32[]{:S(2)}) copy-start(f32[256]{0:T(256)} %copy-done.13) | copy-start | bytes 3076
  227.9 42.1 %copy-start.4 = (f32[1,1,1,512,256]{4,3,2,1,0:T(8,128)S(1)}, f32[1,1,1,512,256]{4,3,2,1,0:T(8,128)}, u32[]{:S(2)}) copy-start(f32[1,1,1,512,256]{4,3,2,1,0:T(8,128)} %get-tuple-element.14) | copy-start | bytes 1572868
  227.9 42.1 %copy-start.7 = (f32[1,1,1,512,256]{4,3,2,1,0:T(8,128)S(1)}, f32[1,1,1,512,256]{4,3,2,1,0:T(8,128)}, u32[]{:S(2)}) copy-start(f32[1,1,1,512,256]{4,3,2,1,0:T(8,128)} %get-tuple-element.21) | copy-start | bytes 1572868
  227.9 42.1 %copy-start.8 = (f32[1,1,1,512,256]{4,3,2,1,0:T(8,128)S(1)}, f32[1,1,1,512,256]{4,3,2,1,0:T(8,128)}, u32[]{:S(2)}) copy-start(f32[1,1,1,512,256]{4,3,2,1,0:T(8,128)} %get-tuple-element.9) | copy-start | bytes 1572868
  227.9 42.2 %copy-start.9 = (f32[1,1,1,512,256]{4,3,2,1,0:T(8,128)S(1)}, f32[1,1,1,512,256]{4,3,2,1,0:T(8,128)}, u32[]{:S(2)}) copy-start(f32[1,1,1,512,256]{4,3,2,1,0:T(8,128)} %get-tuple-element.20) | copy-start | bytes 1572868
  (9 other events, 80.3 us)
